TPU v7x, 256 devices: a whole 4x4x8 slice. The times are simulated.
256 devices in a mesh: ctx: 32 (over y, x, core), tp: 8 (over z).
Axes of the slice: x: 4, y: 4, z: 8, core: 2. Of those that a mesh axis runs over, the one named last changes fastest.
Arguments:
- queries: bfloat16 [8192, 4096], P('ctx', 'tp'), may hold values from -12 to 12, as said below
- key_rows: bfloat16 [8192, 1024], P('ctx', 'tp'), may hold values from -12 to 12, as said below
- value_rows: bfloat16 [8192, 1024], P('ctx', 'tp'), may hold values from -6 to 6
- segments: int32 [8192], replicated, may hold values from 0 to 63, never falling along the last dimension, each value on 1 to 4096 neighbouring positions
- owner_ids: int32 [8192, 1], P('ctx'), may hold values from 0 to 7; in each aligned block of 256 rows (0 to 255, 256 to 511, ...) at most 64 rows name the same one
- out_proj: bfloat16 [4096, 8192], P('tp'), may hold values from -0.09375 to 0.09375
- residual: bfloat16 [16384, 8192], P(('ctx', 'tp')), may hold values from -4 to 4
- norm_gain: float32 [8192], replicated, may hold values from 0.5 to 1.5
Outputs:
- hidden_out: bfloat16 [16384, 8192], P(('ctx', 'tp'))
- normed: bfloat16 [16384, 8192], P(('ctx', 'tp'))
Inputs may be any that keep to these rules, and one draw needn't show every extreme that they name: `segments`: never falling along the tokens; every document has 1 to 4096 tokens and one has exactly 4096. `owner_ids`: among the rows of one device's token block no owner is named more than 64 times; some owner is named exactly 64 times in some block. `queries`: Real-valued entries. `key_rows`: Real-valued entries.
All inputs are finite; a program needn't handle non-finite values.
Results may differ from a plain program's by a relative error of at most 0.01.
Values may be sent and summed in bfloat16 or wider, within the bound.
No kernel may reach another device: no remote copies, remote signals or barrier semaphores. Data moves between devices by JAX's collectives and lax.ppermute only.
A program may use at most 128 MiB of HBM per device.

v0:
```python
import math
import jax
import jax.numpy as jnp
from jax import lax
from jax.sharding import PartitionSpec as P

HEADS = 32
KV_HEADS = 8
HEAD_DIM = 128


def slot_sources(owners, row_rank, owner_here, slot_count):
    token_count = owners.shape[0]
    slot_numbers = jnp.arange(slot_count, dtype=jnp.int32)[:, None]
    matches = ((owners[None, :] == owner_here) & (row_rank[None, :] == slot_numbers)).astype(
        jnp.int32
    )
    token_index = jnp.sum(matches * jnp.arange(token_count, dtype=jnp.int32)[None, :], axis=1)
    filled = jnp.sum(matches, axis=1) > 0
    return (token_index, filled)


def on_device(queries, key_rows, value_rows, segments, owner_ids, out_proj, residual, norm_gain):
    rows_here = queries.shape[0]
    kv_local = key_rows.shape[1] // HEAD_DIM
    group_size = HEADS // KV_HEADS
    score_scale = 1.0 / math.sqrt(HEAD_DIM)
    my_start = lax.axis_index("ctx") * rows_here
    query_heads = queries.reshape(rows_here, kv_local, group_size, HEAD_DIM)
    query_pos = my_start + jnp.arange(rows_here, dtype=jnp.int32)
    query_seg = lax.dynamic_slice_in_dim(segments, my_start, rows_here, 0)
    start_state = (
        jnp.full((kv_local, group_size, rows_here), -1e30, jnp.float32),
        jnp.zeros((kv_local, group_size, rows_here), jnp.float32),
        jnp.zeros((kv_local, group_size, rows_here, HEAD_DIM), jnp.float32),
    )
    carried = start_state
    key_piece = lax.all_gather(key_rows, "ctx", axis=0, tiled=True)
    value_piece = lax.all_gather(value_rows, "ctx", axis=0, tiled=True)
    piece_rows = key_piece.shape[0]
    key_width = 512
    block_count = piece_rows // key_width
    key_blocks = key_piece.reshape(block_count, key_width, kv_local, HEAD_DIM)
    value_blocks = value_piece.reshape(block_count, key_width, kv_local, HEAD_DIM)

    def update(states, block_item):
        block_index, key_block, value_block = block_item
        key_start = block_index * key_width
        key_seg = lax.dynamic_slice_in_dim(segments, key_start, key_width, 0)
        key_pos = key_start + jnp.arange(key_width, dtype=jnp.int32)
        allowed = (query_seg[:, None] == key_seg[None, :]) & (
            key_pos[None, :] <= query_pos[:, None]
        )
        running_max, totals, weighted = states
        scores = (
            jnp.einsum("tkgd,skd->kgts", query_heads, key_block, preferred_element_type=jnp.float32)
            * score_scale
        )
        scores = jnp.where(allowed, scores, -1e30)
        new_max = jnp.maximum(running_max, jnp.max(scores, axis=-1))
        exponent = jnp.where(allowed, jnp.exp(scores - new_max[..., None]), 0.0)
        factor = jnp.exp(running_max - new_max)
        totals = totals * factor + jnp.sum(exponent, axis=-1)
        weighted = weighted * factor[..., None] + jnp.einsum(
            "kgts,skd->kgtd",
            exponent.astype(jnp.bfloat16),
            value_block,
            preferred_element_type=jnp.float32,
        )
        states = (new_max, totals, weighted)
        return (states, None)

    carried, _ = lax.scan(
        update, carried, (jnp.arange(block_count, dtype=jnp.int32), key_blocks, value_blocks)
    )
    running_max, totals, weighted = carried
    mixed_heads = weighted / totals[..., None]
    attended = jnp.transpose(mixed_heads, (2, 0, 1, 3)).reshape(rows_here, -1).astype(jnp.bfloat16)
    partial_rows = jnp.dot(attended, out_proj, preferred_element_type=jnp.float32).astype(
        jnp.bfloat16
    )
    slot_count = residual.shape[0]
    owner_count = lax.axis_size("tp")
    owner_here = lax.axis_index("tp")
    owners = owner_ids[:, 0]
    onehot = (owners[:, None] == jnp.arange(owner_count, dtype=jnp.int32)[None, :]).astype(
        jnp.int32
    )
    before = jnp.cumsum(onehot, axis=0) - onehot
    row_rank = jnp.sum(before * onehot, axis=1)
    summed = lax.psum(partial_rows.astype(jnp.float32).astype(jnp.bfloat16), "tp").astype(
        jnp.float32
    )
    token_index, filled = slot_sources(owners, row_rank, owner_here, slot_count)
    owned_rows = jnp.where(filled[:, None], jnp.take(summed, token_index, axis=0), 0.0)
    hidden_sum = residual.astype(jnp.float32) + owned_rows
    mean_square = jnp.mean(hidden_sum * hidden_sum, axis=-1, keepdims=True)
    normed = hidden_sum * lax.rsqrt(mean_square + 1e-05) * norm_gain
    return (hidden_sum.astype(jnp.bfloat16), normed.astype(jnp.bfloat16))


def solution(mesh):
    placed = (
        P("ctx", "tp"),
        P("ctx", "tp"),
        P("ctx", "tp"),
        P(),
        P("ctx", None),
        P("tp", None),
        P(("ctx", "tp"), None),
        P(),
    )
    return jax.shard_map(
        on_device,
        mesh=mesh,
        in_specs=placed,
        out_specs=(P(("ctx", "tp"), None), P(("ctx", "tp"), None)),
        check_vma=False,
    )
```

profile of v0, /device:TPU:1, one launch (start us, length us, event | category | flops | bytes accessed | tf_op | source)
XLA Modules:
  0.0 347.0 jit_solution(442870078505631397)
XLA Ops:
  10.8 52.6 %all-gather.3.cloned.1.call-done = bf16[8192,128]{1,0:T(8,128)(2,1)} async-done(((bf16[256,128]{1,0:T(8,128)(2,1)}), bf16[8192,128]{1,0:T(8,128)(2,1)}) %all-gather.3.cloned.1.call-update) | async-done | bytes 2097168 | tf_op jit(solution)/shard_map/all_gather | solution.py:38
  63.3 50.6 %all-gather.5.cloned.1.call-done = bf16[8192,128]{1,0:T(8,128)(2,1)} async-done(((bf16[256,128]{1,0:T(8,128)(2,1)}), bf16[8192,128]{1,0:T(8,128)(2,1)}) %all-gather.5.cloned.1.call-update) | async-done | bytes 2097168 | tf_op jit(solution)/shard_map/all_gather | solution.py:39
  113.9 95.9 %while.15 = (s32[]{:T(128)}, f32[1,4,256]{2,1,0:T(4,128)S(1)}, f32[1,4,256]{2,1,0:T(4,128)S(1)}, f32[1,4,256,128]{3,2,1,0:T(8,128)S(1)}, s32[256]{0:T(256)S(1)},...) while((s32[]{:T(128)}, f32[1,4,256]{2,1,0:T(4,128)S(1)}, ...), condition=%wide.region_8.9_spmd.clone, body=%wide.region_5.8_spmd.clone.sunk | while | flops 276044544 | bytes 8468703 | solution.py:73
  117.5 1.8 fusion.44
  123.5 1.8 fusion.44
  128.1 1.4 fusion.41
  129.5 1.8 fusion.44
  134.1 1.4 fusion.41
  135.5 1.8 fusion.44
  140.1 1.4 fusion.41
  141.5 1.8 fusion.44
  146.1 1.4 fusion.41
  147.5 1.8 fusion.44
  152.1 1.4 fusion.41
  153.5 1.8 fusion.44
  158.1 1.4 fusion.41
  159.5 1.8 fusion.44
  164.1 1.4 fusion.41
  165.5 1.8 fusion.44
  170.1 1.4 fusion.41
  171.5 1.8 fusion.44
  177.5 1.8 fusion.44
  183.5 1.8 fusion.44
  189.5 1.8 fusion.44
  195.5 1.8 fusion.44
  201.5 1.8 fusion.44
  207.5 1.8 fusion.44
  210.1 7.7 %convolution_convert_fusion = bf16[256,8192]{1,0:T(8,128)(2,1)} fusion(bf16[256,512]{0,1:T(8,128)(2,1)S(1)} %bitcast.97, bf16[512,8192]{1,0:T(8,128)(2,1)} %param.15), kind=kOutput, calls=%fused_computation.35 | convolution fusion | flops 2149580800 | bytes 12845056 | tf_op jit(solution)/shard_map/dot_general | solution.py:79
  219.6 106.2 %all-reduce.2.cloned.1.call-done = bf16[256,8192]{1,0:T(8,128)(2,1)} async-done(((bf16[256,8192]{1,0:T(8,128)(2,1)}), bf16[256,8192]{1,0:T(8,128)(2,1)}) %all-reduce.2.cloned.1.call-update) | async-done | bytes 4194320 | tf_op jit(solution)/shard_map/psum | solution.py:91
  325.7 6.4 %convert_element_type.47 = f32[256,8192]{1,0:T(8,128)} convert(bf16[256,8192]{1,0:T(8,128)(2,1)} %all-reduce.2.cloned.1.call-done) | non-fusion elementwise | flops 2097152 | bytes 12582912 | tf_op jit(solution)/shard_map/convert_element_type | solution.py:91
  332.1 5.7 %gather_fusion = f32[64,8192]{1,0:T(8,128)S(1)} fusion(f32[256,8192]{1,0:T(8,128)} %convert_element_type.47, s32[1024]{0:T(1024)S(1)} %pad_clamp_fusion), kind=kCustom, calls=%fused_computation | custom fusion | bytes 4194560 | tf_op jit(solution)/shard_map/jit(_take)/gather | solution.py:95
  338.6 1.9 multiply_convert_fusion
  (186 shorter events, 51.5 us)
Async XLA Ops:
  7.2 56.2 %all-gather.3.cloned.1.call-start = ((), (), s32[]{:S(2)}) async-start(), calls=%async_computation | async-start | bytes 2162688 | tf_op jit(solution)/shard_map/all_gather | solution.py:38
  7.9 106.0 %all-gather.5.cloned.1.call-start = ((), (), s32[]{:S(2)}) async-start(), calls=%async_computation.1 | async-start | bytes 2162688 | tf_op jit(solution)/shard_map/all_gather | solution.py:39
  8.6 317.1 %all-reduce.2.cloned.1.call-start = ((), (), s32[]{:S(2)}) async-start(), calls=%async_computation.2 | async-start | bytes 8388608 | tf_op jit(solution)/shard_map/psum | solution.py:91
  217.8 0.7 copy-start.2
  332.1 5.7 %copy-start = (bf16[64,8192]{1,0:T(8,128)(2,1)S(1)}, bf16[64,8192]{1,0:T(8,128)(2,1)}, u32[]{:S(2)}) copy-start(bf16[64,8192]{1,0:T(8,128)(2,1)} %param.16) | copy-start | bytes 3145732
  337.8 0.8 copy-start.1
Sparse Core Ops, SparseCore 0:
  10.5 52.7 all-gather.2
  65.9 47.9 all-gather.4
  217.9 107.7 all-reduce.1
where the time goes:
time: 349 us; the launch traced here: 347 us
  waiting for transfers between devices  211 us (60%)
  matrix products  58.6 us (17%)
  local copies, waits for them, and re-layouts  30.7 us (9%)
  other arithmetic  22.1 us (6%)
  between operations  13.9 us (4%)
  loops' own time  10.9 us (3%)
    psum x1, waiting for transfers between devices, on_device(): lax.psum(partial_rows.astype(jnp.float32).astype(jnp.bfloat16), 'tp')  106 us
    all_gather x1, waiting for transfers between devices, on_device(): key_piece = lax.all_gather(key_rows, 'ctx', axis=0, tiled=True)  52.6 us
    all_gather x1, waiting for transfers between devices, on_device(): value_piece = lax.all_gather(value_rows, 'ctx', axis=0, tiled=True)  50.6 us
    dot_general x16, matrix products, update(): jnp.einsum('kgts,skd->kgtd', exponent.astype(jnp.bfloat16), value_block,...  28.7 us
    dot_general x16, matrix products, update(): jnp.einsum('tkgd,skd->kgts', query_heads, key_block, preferred_element_ty...  22.3 us
    dynamic_slice x16, local copies, waits for them, and re-layouts, update(): key_seg = lax.dynamic_slice_in_dim(segments, key_start, key_width, 0)  12.2 us
    another operation x1, loops' own time, on_device(): lax.scan(update, carried, (jnp.arange(block_count, dtype=jnp.int32), key_...  10.9 us
    dynamic_slice x16, local copies, waits for them, and re-layouts, on_device(): lax.scan(update, carried, (jnp.arange(block_count, dtype=jnp.int32), key_...  9.51 us
  transfers between devices with their start and end apart: 3, of which 3 were waited for; matrix products, arithmetic and copies ran while one was open for 1% of the time, Pallas kernels for 0%

commit v1 on v0

--- a/solution.py
+++ b/solution.py
@@ -1,3 +1,4 @@
+import functools
 import math
 import jax
 import jax.numpy as jnp
@@ -7,6 +8,19 @@
 HEADS = 32
 KV_HEADS = 8
 HEAD_DIM = 128
+
+
+def _post_cube(field, comm_axis):
+    runs = []
+    for _ in range(lax.psum(1, comm_axis)):
+        runs.append(field)
+    right_arr = jnp.concatenate(
+        lax.all_to_all(jnp.stack(runs, axis=0), axis_name=comm_axis, split_axis=0, concat_axis=0), 0
+    )
+    return right_arr
+
+
+bench_part = functools.partial(_post_cube, comm_axis="ctx")
 
 
 def slot_sources(owners, row_rank, owner_here, slot_count):
@@ -36,7 +50,7 @@
     )
     carried = start_state
     key_piece = lax.all_gather(key_rows, "ctx", axis=0, tiled=True)
-    value_piece = lax.all_gather(value_rows, "ctx", axis=0, tiled=True)
+    value_piece = bench_part(value_rows)
     piece_rows = key_piece.shape[0]
     key_width = 512
     block_count = piece_rows // key_width

time: 349 us -> 309 us (0.89)
  waiting for transfers between devices: 211 us -> 160 us
  starting transfers between devices: 0.11 us -> 8.84 us
    all_gather x1 -> x0, waiting for transfers between devices: 50.6 us -> none  [on_device(): value_piece = lax.all_gather(value_rows, 'ctx', axis=0, tiled=True)]
    all_to_all x0 -> x1, waiting for transfers between devices: none -> 28.3 us  [_post_cube(): lax.all_to_all(jnp.stack(runs, axis=0), axis_name=comm_axis, split_axis=0...]
    all_gather x1, waiting for transfers between devices: 52.6 us -> 25 us  [on_device(): key_piece = lax.all_gather(key_rows, 'ctx', axis=0, tiled=True)]
    all_to_all x0 -> x1, starting transfers between devices: none -> 8.76 us  [_post_cube(): lax.all_to_all(jnp.stack(runs, axis=0), axis_name=comm_axis, split_axis=0...]
  transfers between devices with their start and end apart: 3 -> 3, of which waited for: 3 -> 3; matrix products, arithmetic and copies ran while one was open for 1% -> 2% of each run, Pallas kernels for 0% -> 0%
where the time goes in v1:
time: 309 us; the launch traced here: 307 us
  waiting for transfers between devices  160 us (52%)
  matrix products  58.4 us (19%)
  local copies, waits for them, and re-layouts  32.4 us (10%)
  other arithmetic  22.1 us (7%)
  between operations  14.2 us (5%)
  loops' own time  10.9 us (4%)
  starting transfers between devices  8.84 us (3%)
    psum x1, waiting for transfers between devices, on_device(): lax.psum(partial_rows.astype(jnp.float32).astype(jnp.bfloat16), 'tp')  106 us
    dot_general x16, matrix products, update(): jnp.einsum('kgts,skd->kgtd', exponent.astype(jnp.bfloat16), value_block,...  28.4 us
    all_to_all x1, waiting for transfers between devices, _post_cube(): lax.all_to_all(jnp.stack(runs, axis=0), axis_name=comm_axis, split_axis=0...  28.3 us
    all_gather x1, waiting for transfers between devices, on_device(): key_piece = lax.all_gather(key_rows, 'ctx', axis=0, tiled=True)  25 us
    dot_general x16, matrix products, update(): jnp.einsum('tkgd,skd->kgts', query_heads, key_block, preferred_element_ty...  22.2 us
    dynamic_slice x16, local copies, waits for them, and re-layouts, update(): key_seg = lax.dynamic_slice_in_dim(segments, key_start, key_width, 0)  12.2 us
    another operation x1, loops' own time, on_device(): lax.scan(update, carried, (jnp.arange(block_count, dtype=jnp.int32), key_...  10.9 us
    dynamic_slice x16, local copies, waits for them, and re-layouts, on_device(): lax.scan(update, carried, (jnp.arange(block_count, dtype=jnp.int32), key_...  9.51 us
  transfers between devices with their start and end apart: 3, of which 3 were waited for; matrix products, arithmetic and copies ran while one was open for 2% of the time, Pallas kernels for 0%

profile of v1, /device:TPU:1, one launch (start us, length us, event | category | flops | bytes accessed | tf_op | source)
XLA Modules:
  0.0 307.0 jit_solution(11400248227723913571)
XLA Ops:
  7.9 2.6 stack.2
  10.5 8.8 %all-to-all-start = ((bf16[32,256,128]{2,1,0:T(8,128)(2,1)}), bf16[32,256,128]{2,1,0:T(8,128)(2,1)}, u32[]{:S(2)}, u32[]{:S(2)}) async-start(bf16[32,256,128]{2,1,0:T(8,128)(2,1)} %stack.2), calls=%async_computation | async-start | bytes 4194304 | tf_op jit(solution)/shard_map/all_to_all | solution.py:18
  20.5 28.3 %all-to-all-done = bf16[32,256,128]{2,1,0:T(8,128)(2,1)} async-done(((bf16[32,256,128]{2,1,0:T(8,128)(2,1)}), bf16[32,256,128]{2,1,0:T(8,128)(2,1)}, u32[]{:S(2)}, u32[]{:S(2)}) %all-to-all-start) | async-done | bytes 2097184 | tf_op jit(solution)/shard_map/all_to_all | solution.py:18
  48.8 25.0 %all-gather.2.cloned.1.call-done = bf16[8192,128]{1,0:T(8,128)(2,1)} async-done(((bf16[256,128]{1,0:T(8,128)(2,1)}), bf16[8192,128]{1,0:T(8,128)(2,1)}) %all-gather.2.cloned.1.call-update) | async-done | bytes 2097168 | tf_op jit(solution)/shard_map/all_gather | solution.py:52
  73.8 95.6 %while.15 = (s32[]{:T(128)}, f32[1,4,256]{2,1,0:T(4,128)S(1)}, f32[1,4,256]{2,1,0:T(4,128)S(1)}, f32[1,4,256,128]{3,2,1,0:T(8,128)S(1)}, s32[256]{0:T(256)S(1)},...) while((s32[]{:T(128)}, f32[1,4,256]{2,1,0:T(4,128)S(1)}, ...), condition=%wide.region_8.9_spmd.clone, body=%wide.region_5.8_spmd.clone.sunk | while | flops 276044544 | bytes 8468703 | solution.py:87
  77.4 1.8 fusion.44
  83.4 1.8 fusion.44
  89.4 1.8 fusion.44
  95.4 1.8 fusion.44
  99.9 1.4 fusion.41
  101.3 1.8 fusion.44
  107.3 1.8 fusion.44
  111.9 1.4 fusion.41
  113.3 1.8 fusion.44
  119.3 1.8 fusion.44
  123.8 1.4 fusion.41
  125.3 1.8 fusion.44
  131.2 1.8 fusion.44
  135.8 1.4 fusion.41
  137.2 1.8 fusion.44
  143.2 1.8 fusion.44
  147.8 1.4 fusion.41
  149.2 1.8 fusion.44
  155.2 1.8 fusion.44
  159.7 1.4 fusion.41
  161.1 1.8 fusion.44
  167.1 1.8 fusion.44
  169.7 7.7 %convolution_convert_fusion = bf16[256,8192]{1,0:T(8,128)(2,1)} fusion(bf16[256,512]{0,1:T(8,128)(2,1)S(1)} %bitcast.97, bf16[512,8192]{1,0:T(8,128)(2,1)} %param.15), kind=kOutput, calls=%fused_computation.35 | convolution fusion | flops 2149580800 | bytes 12845056 | tf_op jit(solution)/shard_map/dot_general | solution.py:93
  179.2 106.2 %all-reduce.2.cloned.1.call-done = bf16[256,8192]{1,0:T(8,128)(2,1)} async-done(((bf16[256,8192]{1,0:T(8,128)(2,1)}), bf16[256,8192]{1,0:T(8,128)(2,1)}) %all-reduce.2.cloned.1.call-update) | async-done | bytes 4194320 | tf_op jit(solution)/shard_map/psum | solution.py:105
  285.4 6.4 %convert_element_type.47 = f32[256,8192]{1,0:T(8,128)} convert(bf16[256,8192]{1,0:T(8,128)(2,1)} %all-reduce.2.cloned.1.call-done) | non-fusion elementwise | flops 2097152 | bytes 12582912 | tf_op jit(solution)/shard_map/convert_element_type | solution.py:105
  291.8 5.7 %gather_fusion = f32[64,8192]{1,0:T(8,128)S(1)} fusion(f32[256,8192]{1,0:T(8,128)} %convert_element_type.47, s32[1024]{0:T(1024)S(1)} %pad_clamp_fusion), kind=kCustom, calls=%fused_computation | custom fusion | bytes 4194560 | tf_op jit(solution)/shard_map/jit(_take)/gather | solution.py:109
  298.2 1.9 multiply_convert_fusion
  (188 shorter events, 52.6 us)
Async XLA Ops:
  7.2 66.6 %all-gather.2.cloned.1.call-start = ((), (), s32[]{:S(2)}) async-start(), calls=%async_computation.1 | async-start | bytes 2162688 | tf_op jit(solution)/shard_map/all_gather | solution.py:52
  10.5 8.9 %copy-start.1 = (bf16[256,512]{1,0:T(8,128)(2,1)S(1)}, bf16[256,512]{1,0:T(8,128)(2,1)}, u32[]{:S(2)}) copy-start(bf16[256,512]{1,0:T(8,128)(2,1)} %param.10) | copy-start | bytes 786436
  10.5 38.3 %all-to-all-start = ((bf16[32,256,128]{2,1,0:T(8,128)(2,1)}), bf16[32,256,128]{2,1,0:T(8,128)(2,1)}, u32[]{:S(2)}, u32[]{:S(2)}) async-start(bf16[32,256,128]{2,1,0:T(8,128)(2,1)} %stack.2), calls=%async_computation | async-start | bytes 4194304 | tf_op jit(solution)/shard_map/all_to_all | solution.py:18
  19.3 266.1 %all-reduce.2.cloned.1.call-start = ((), (), s32[]{:S(2)}) async-start(), calls=%async_computation.2 | async-start | bytes 8388608 | tf_op jit(solution)/shard_map/psum | solution.py:105
  177.4 0.7 copy-start.3
  291.8 5.7 %copy-start = (bf16[64,8192]{1,0:T(8,128)(2,1)S(1)}, bf16[64,8192]{1,0:T(8,128)(2,1)}, u32[]{:S(2)}) copy-start(bf16[64,8192]{1,0:T(8,128)(2,1)} %param.16) | copy-start | bytes 3145732
  297.5 0.8 copy-start.2
Sparse Core Ops, SparseCore 0:
  10.5 63.2 all-gather.1
  177.6 107.8 all-reduce.1
